TPU v7x, 128 devices: a whole 4x4x4 slice. The times are simulated.
128 devices in a mesh: wl: 8 (over x, z_hi), tile: 16 (over z_lo, y, core).
Axes of the slice: x: 4, y: 4, z: 4 (z_hi: 2, z_lo: 2; z = z_hi * 2 + z_lo), core: 2. Of those that a mesh axis runs over, the one named last changes fastest.
Arguments:
- density: float32 [32, 1024], P('tile', 'wl'), may hold values from 0 to 1
- foot_index: int32 [4, 128, 4096], P(None, 'tile'), may hold values from 0 to 2047, as said below
- foot_weight: bfloat16 [4, 128, 4096], P(None, 'tile'), may hold values from 0.099609375 to 0.3984375
- source_fwd: float32 [16, 128, 4096], P('wl', 'tile'), may hold values from -6 to 6
- source_adj: float32 [16, 128, 4096], P('wl', 'tile'), may hold values from -6 to 6
- omega: float32 [16], P('wl'), may hold values from 0.2 to 1.5
Outputs:
- forward_field: float32 [16, 128, 4096], P('wl', 'tile')
- density_grad: float32 [32, 1024], P('tile', 'wl')
Inputs may be any that keep to these rules, and one draw needn't show every extreme that they name: foot_index[f, x, y] = r * 1024 + c names coarse row r and column c of the strip of the tile holding row x, with r within one of (x mod 8) // 4 and c within two of y // 4; entry f = 0 is the cell's own block.
All inputs are finite; a program needn't handle non-finite values.
Results may differ from a plain program's by a relative error of at most 0.0003.
Values sent between devices are 32-bit elements; how exact they have to be, the bound alone decides.
No kernel may reach another device: no remote copies, remote signals or barrier semaphores. Data moves between devices by JAX's collectives and lax.ppermute only.
A program may use at most 192 MiB of HBM per device.

v0:
```python
import jax
import jax.numpy as jnp
from jax import lax
from jax.sharding import PartitionSpec as P

ITERS = 4
HALO = 4
SHIFTS = (-2, -1, 0, 1, 2)
time_step = 0.5
high_contrast = 4.0
drude_decay = 0.9
drude_gain = 0.5


def from_behind(value, axis, steps):
    count = lax.axis_size(axis)
    first, last = (max(0, -steps), min(count, count - steps))
    return lax.ppermute(value, axis, [(source, source + steps) for source in range(first, last)])


def with_halo(value, axis):
    above = from_behind(value[..., -HALO:, :], axis, 1)
    below = from_behind(value[..., :HALO, :], axis, -1)
    return jnp.concatenate([above, value, below], axis=-2)


def lane_shift(vector, shift):
    width = vector.shape[-1]
    pad = [(0, 0)] * (vector.ndim - 1) + [(abs(shift), abs(shift))]
    padded = jnp.pad(vector, pad)
    start = abs(shift) - shift
    return lax.slice_in_dim(padded, start, start + width, axis=vector.ndim - 1)


def march(source, drive, density_cell, inverse, valid):
    field_e = jnp.zeros_like(source)
    field_hx = jnp.zeros_like(source)
    field_hy = jnp.zeros_like(source)
    current = jnp.zeros_like(source)
    rows = source.shape[2]
    history = []
    for turn in range(ITERS):
        row_zero = jnp.zeros_like(source[:, :, :1, :])
        col_zero = jnp.zeros_like(source[:, :, :, :1])
        e_up = jnp.concatenate([field_e[:, :, 1:, :], row_zero], 2)
        e_right = jnp.concatenate([field_e[:, :, :, 1:], col_zero], 3)
        field_hx = field_hx - time_step * (e_right - field_e)
        field_hy = (field_hy + time_step * (e_up - field_e)) * valid
        current = drude_decay * current + drude_gain * density_cell * field_e
        hy_down = jnp.concatenate([row_zero, field_hy[:, :, :-1, :]], 2)
        hx_left = jnp.concatenate([col_zero, field_hx[:, :, :, :-1]], 3)
        field_e = (
            field_e
            + inverse * (field_hy - hy_down - (field_hx - hx_left) - current)
            + drive[turn] * source
        ) * valid
        history.append(field_e[:, :, HALO : rows - HALO, :])
    return history


def shards(density, foot_index, foot_weight, source_fwd, source_adj, omega):
    sources = jnp.stack([source_fwd, source_adj])
    sources_ext = with_halo(sources, "tile")
    strip = lax.all_gather(density, "wl", axis=1, tiled=True)
    block_rows, block_cols = strip.shape
    cells_x, cells_y = foot_index.shape[1:]
    factor = cells_y // block_cols
    weights = foot_weight.astype(jnp.float32)
    col_block = lax.broadcasted_iota(jnp.int32, (1, cells_y), 1) // factor
    key = foot_index // block_cols * len(SHIFTS) + (foot_index % block_cols - col_block[None]) + 2
    upsampled = jnp.repeat(strip, factor, axis=1)
    matched = []
    density_cell = jnp.zeros((cells_x, cells_y), jnp.float32)
    for row in range(block_rows):
        for slot, shift in enumerate(SHIFTS):
            code = row * len(SHIFTS) + slot
            weight_sum = jnp.sum(jnp.where(key == code, weights, 0.0), axis=0)
            matched.append(weight_sum)
            density_cell = (
                density_cell + weight_sum * lane_shift(upsampled[row], -factor * shift)[None]
            )
    density_ext = with_halo(density_cell, "tile")
    inverse_ext = time_step / (1.0 + high_contrast * density_ext)
    rows_ext = cells_x + 2 * HALO
    global_row = (
        lax.axis_index("tile") * cells_x - HALO + lax.broadcasted_iota(jnp.int32, (rows_ext, 1), 0)
    )
    valid = ((global_row >= 0) & (global_row < cells_x * lax.axis_size("tile"))).astype(jnp.float32)
    drive = [jnp.sin(omega * (turn + 1.0))[None, :, None, None] for turn in range(ITERS)]
    history = march(sources_ext, drive, density_ext, inverse_ext, valid)
    sense = jnp.zeros((cells_x, cells_y), jnp.float32)
    for turn in range(ITERS):
        sense = sense + jnp.sum(history[turn][1] * history[ITERS - 1 - turn][0], axis=0)
    total_waves = source_fwd.shape[0] * lax.axis_size("wl")
    scaled = high_contrast / total_waves * sense
    pooled_rows = []
    for row in range(block_rows):
        acc = jnp.zeros((cells_y,), jnp.float32)
        for slot, shift in enumerate(SHIFTS):
            per_col = jnp.sum(matched[row * len(SHIFTS) + slot] * scaled, axis=0)
            acc = acc + lane_shift(per_col, factor * shift)
        pooled_rows.append(acc.reshape(block_cols, factor).sum(axis=1))
    partial_grad = jnp.stack(pooled_rows)
    density_grad = lax.psum_scatter(partial_grad, "wl", scatter_dimension=1, tiled=True)
    return (history[ITERS - 1][0], density_grad)


def solution(mesh):
    in_specs = (
        P("tile", "wl"),
        P(None, "tile", None),
        P(None, "tile", None),
        P("wl", "tile", None),
        P("wl", "tile", None),
        P("wl"),
    )
    out_specs = (P("wl", "tile", None), P("tile", "wl"))
    return jax.shard_map(shards, mesh=mesh, in_specs=in_specs, out_specs=out_specs, check_vma=False)
```

profile of v0, /device:TPU:0, one launch (start us, length us, event | category | flops | bytes accessed | tf_op | source)
XLA Modules:
  0.0 138.3 jit_solution(15025737107666634582)
XLA Ops:
  7.2 0.0 copy-start.4
  7.2 0.0 reduce-scatter.4.cloned.1.call-start
  7.2 0.6 copy-done.4
  7.8 24.2 %all_gather.3 = f32[2,1024]{1,0:T(2,128)S(1)} all-gather(f32[2,128]{1,0:T(2,128)S(1)} %copy-done.4), channel_id=1, replica_groups=mesh['wl'=8,'tile'=16] {'wl'}, dimensions={1}, use_global_device_ids=true | all-gather | bytes 9216 | tf_op jit(solution)/shard_map/all_gather | solution.py:64
  32.1 0.2 broadcast_in_dim.24
  32.3 0.3 broadcast_in_dim.25
  32.6 0.0 copy-start.2
  32.6 0.2 broadcast_in_dim.22
  32.8 0.0 copy-start.3
  32.8 0.3 broadcast_in_dim.23
  33.1 0.1 pad_slice_fusion.5
  33.2 0.5 copy-done.2
  33.6 0.2 copy-done.3
  33.8 1.1 fusion.4
  34.8 0.0 copy-start.1
  34.8 0.1 multiply_add_fusion.2
  35.0 0.0 copy-start
  35.0 1.4 %collective-permute-start.1 = (f32[4,4096]{1,0:T(4,128)S(1)}, f32[4,4096]{1,0:T(4,128)S(1)}, u32[]{:S(2)}, u32[]{:S(2)}) collective-permute-start(f32[4,4096]{1,0:T(4,128)S(1)} %get-tuple-element.38), channel_id=1, source_target_pairs={{1,0},{2,1},{3,2},{4,3},{5,4},{6,5},{7,6},{8,7},{9,8},{10,9},{11,1... | collective-permute-start | bytes 196616 | tf_op jit(solution)/shard_map/ppermute | solution.py:18
  36.5 3.0 %collective-permute-start = (f32[4,4096]{1,0:T(4,128)S(1)}, f32[4,4096]{1,0:T(4,128)S(1)}, u32[]{:S(2)}, u32[]{:S(2)}) collective-permute-start(f32[4,4096]{1,0:T(4,128)S(1)} %get-tuple-element.37), channel_id=1, source_target_pairs={{0,1},{1,2},{2,3},{3,4},{4,5},{5,6},{6,7},{7,8},{8,9},{9,10},{10,1... | collective-permute-start | bytes 196616 | tf_op jit(solution)/shard_map/ppermute | solution.py:18
  39.5 0.0 copy-done.1
  39.5 0.0 copy-done
  39.5 0.1 fusion.18
  39.6 1.3 collective-permute-start.3
  40.9 3.7 %collective-permute-start.2 = (f32[2,2,4,4096]{3,2,1,0:T(4,128)S(1)}, f32[2,2,4,4096]{3,2,1,0:T(4,128)S(1)}, u32[]{:S(2)}, u32[]{:S(2)}) collective-permute-start(f32[2,2,4,4096]{3,2,1,0:T(4,128)S(1)} %get-tuple-element.32), channel_id=1, source_target_pairs={{0,1},{1,2},{2,3},{3,4},{4,5},{5,6},{6,7},{7,8},{8,9},{9,10},{10,1... | collective-permute-start | bytes 786440 | tf_op jit(solution)/shard_map/ppermute | solution.py:18
  44.7 0.0 copy-start.5
  44.7 0.6 copy-done.5
  45.3 0.1 multiply_sine_fusion
  45.4 0.1 pad_subtract_fusion
  45.5 0.1 pad_subtract_fusion.1
  45.6 0.0 collective-permute-done.1
  45.6 0.0 collective-permute-done
  45.6 0.1 broadcast_multiply_fusion.1
  45.7 0.0 collective-permute-done.3
  45.7 0.1 collective-permute-done.2
  45.8 0.3 add_multiply_fusion.6
  46.1 0.1 slice.288
  46.2 0.3 slice.290
  46.5 0.6 add_multiply_fusion.5
  47.1 0.9 add_multiply_fusion.4
  48.0 0.1 slice.292
  48.1 0.3 slice.294
  48.4 0.4 add_multiply_fusion.3
  48.9 1.0 add_multiply_fusion.2
  49.9 0.1 slice.296
  50.0 0.3 slice.298
  50.3 0.4 add_multiply_fusion.1
  50.7 1.1 add_multiply_fusion
  51.9 0.8 fusion.23
  52.6 0.1 fusion.19
  52.7 0.1 fusion.21
  52.8 0.4 multiply_reduce_fusion.5
  53.2 0.1 fusion.31
  53.3 0.5 add.288
  53.9 0.2 reduce_sum.259
  54.1 0.1 fusion.27
  54.2 0.5 add.283
  54.7 0.2 reduce_sum.253
  54.9 1.0 copy.8
  56.0 0.0 reduce-scatter.4.cloned.1.call-update
  56.0 74.0 %reduce-scatter.4.cloned.1.call-done = f32[128,2]{1,0:T(8,128)} async-done(((f32[1024,2]{1,0:T(8,128)}), f32[128,2]{1,0:T(8,128)}) %reduce-scatter.4.cloned.1.call-update) | async-done | bytes 1040
  130.0 1.5 %copy.9 = f32[2,128]{1,0:T(2,128)} copy(f32[2,128]{0,1:T(8,128)} %bitcast.45) | data formatting | bytes 2048
  (9 shorter events, 0.1 us)
Async XLA Ops:
  7.2 0.7 copy-start.4
  7.2 122.8 %reduce-scatter.4.cloned.1.call-start = ((), (), s32[]{:S(2)}) async-start(), calls=%async_computation.1 | async-start | bytes 589824
  32.6 1.0 copy-start.2
  32.8 1.0 copy-start.3
  34.8 4.7 %copy-start.1 = (f32[2,8,4096]{2,1,0:T(8,128)S(1)}, f32[2,8,4096]{2,1,0:T(8,128)}, u32[]{:S(2)}) copy-start(f32[2,8,4096]{2,1,0:T(8,128)} %param.10) | copy-start | bytes 786436
  35.0 4.5 %copy-start = (f32[2,8,4096]{2,1,0:T(8,128)S(1)}, f32[2,8,4096]{2,1,0:T(8,128)}, u32[]{:S(2)}) copy-start(f32[2,8,4096]{2,1,0:T(8,128)} %param.9) | copy-start | bytes 786436
  35.0 10.6 %collective-permute-start.1 = (f32[4,4096]{1,0:T(4,128)S(1)}, f32[4,4096]{1,0:T(4,128)S(1)}, u32[]{:S(2)}, u32[]{:S(2)}) collective-permute-start(f32[4,4096]{1,0:T(4,128)S(1)} %get-tuple-element.38), channel_id=1, source_target_pairs={{1,0},{2,1},{3,2},{4,3},{5,4},{6,5},{7,6},{8,7},{9,8},{10,9},{11,1... | collective-permute-start | bytes 196616 | tf_op jit(solution)/shard_map/ppermute | solution.py:18
  36.5 9.1 %collective-permute-start = (f32[4,4096]{1,0:T(4,128)S(1)}, f32[4,4096]{1,0:T(4,128)S(1)}, u32[]{:S(2)}, u32[]{:S(2)}) collective-permute-start(f32[4,4096]{1,0:T(4,128)S(1)} %get-tuple-element.37), channel_id=1, source_target_pairs={{0,1},{1,2},{2,3},{3,4},{4,5},{5,6},{6,7},{7,8},{8,9},{9,10},{10,1... | collective-permute-start | bytes 196616 | tf_op jit(solution)/shard_map/ppermute | solution.py:18
  39.6 6.1 %collective-permute-start.3 = (f32[2,2,4,4096]{3,2,1,0:T(4,128)S(1)}, f32[2,2,4,4096]{3,2,1,0:T(4,128)S(1)}, u32[]{:S(2)}, u32[]{:S(2)}) collective-permute-start(f32[2,2,4,4096]{3,2,1,0:T(4,128)S(1)} %get-tuple-element.33), channel_id=1, source_target_pairs={{1,0},{2,1},{3,2},{4,3},{5,4},{6,5},{7,6},{8,7},{9,8},{10,9},{11,1... | collective-permute-start | bytes 786440 | tf_op jit(solution)/shard_map/ppermute | solution.py:18
  40.9 4.9 %collective-permute-start.2 = (f32[2,2,4,4096]{3,2,1,0:T(4,128)S(1)}, f32[2,2,4,4096]{3,2,1,0:T(4,128)S(1)}, u32[]{:S(2)}, u32[]{:S(2)}) collective-permute-start(f32[2,2,4,4096]{3,2,1,0:T(4,128)S(1)} %get-tuple-element.32), channel_id=1, source_target_pairs={{0,1},{1,2},{2,3},{3,4},{4,5},{5,6},{6,7},{7,8},{8,9},{9,10},{10,1... | collective-permute-start | bytes 786440 | tf_op jit(solution)/shard_map/ppermute | solution.py:18
  44.7 0.7 copy-start.5
Sparse Core Ops, SparseCore 0:
  56.1 73.8 reduce-scatter.3
where the time goes:
time: 139 us; the launch traced here: 138 us
  waiting for transfers between devices  74.1 us (53%)
  blocking collectives  24.2 us (17%)
  between operations  14.3 us (10%)
  starting transfers between devices  9.53 us (7%)
  other arithmetic  8.32 us (6%)
  local copies, waits for them, and re-layouts  7.76 us (6%)
    unnamed x2, waiting for transfers between devices  74 us
    all_gather x1, blocking collectives, shards(): strip = lax.all_gather(density, 'wl', axis=1, tiled=True)  24.2 us
    ppermute x4, starting transfers between devices, from_behind(): lax.ppermute(value, axis, [(source, source + steps) for source in range(f...  9.49 us
    unnamed x14, local copies, waits for them, and re-layouts  4.38 us
    mul x4, other arithmetic, march(): (field_e + inverse * (field_hy - hy_down - (field_hx - hx_left) - current...  3.26 us
  transfers between devices with their start and end apart: 5, of which 2 were waited for; matrix products, arithmetic and copies ran while one was open for 0% of the time, Pallas kernels for 0%

commit v1 on v0

--- a/solution.py
+++ b/solution.py
@@ -61,7 +61,9 @@
 def shards(density, foot_index, foot_weight, source_fwd, source_adj, omega):
     sources = jnp.stack([source_fwd, source_adj])
     sources_ext = with_halo(sources, "tile")
-    strip = lax.all_gather(density, "wl", axis=1, tiled=True)
+    strip = jnp.concatenate(
+        lax.all_to_all(jnp.stack([density] * lax.axis_size("wl")), "wl", 0, 0), axis=1
+    )
     block_rows, block_cols = strip.shape
     cells_x, cells_y = foot_index.shape[1:]
     factor = cells_y // block_cols

time: 139 us -> 129 us (0.928)
  blocking collectives: 24.2 us -> 0 us
  starting transfers between devices: 9.53 us -> 17.1 us
  waiting for transfers between devices: 74.1 us -> 79.6 us
    all_gather x1 -> x0, blocking collectives: 24.2 us -> none  [shards(): strip = lax.all_gather(density, 'wl', axis=1, tiled=True)]
    all_to_all x0 -> x1, starting transfers between devices: none -> 7.7 us  [shards(): lax.all_to_all(jnp.stack([density] * lax.axis_size('wl')), 'wl', 0, 0)]
    unnamed x2, waiting for transfers between devices: 74 us -> 78.8 us
    unnamed x14 -> x12, local copies, waits for them, and re-layouts: 4.38 us -> 3.25 us
  transfers between devices with their start and end apart: 5 -> 6, of which waited for: 2 -> 2; matrix products, arithmetic and copies ran while one was open for 0% -> 3% of each run, Pallas kernels for 0% -> 0%
where the time goes in v1:
time: 129 us
  waiting for transfers between devices  79.6 us (62%)
  starting transfers between devices  17.1 us (13%)
  between operations  14.3 us (11%)
  other arithmetic  9.62 us (7%)
  local copies, waits for them, and re-layouts  7.91 us (6%)
    unnamed x2, waiting for transfers between devices  78.8 us
    ppermute x4, starting transfers between devices, from_behind(): lax.ppermute(value, axis, [(source, source + steps) for source in range(f...  9.35 us
    all_to_all x1, starting transfers between devices, shards(): lax.all_to_all(jnp.stack([density] * lax.axis_size('wl')), 'wl', 0, 0)  7.7 us
    mul x4, other arithmetic, march(): (field_e + inverse * (field_hy - hy_down - (field_hx - hx_left) - current...  3.28 us
    unnamed x12, local copies, waits for them, and re-layouts  3.25 us
  transfers between devices with their start and end apart: 6, of which 2 were waited for; matrix products, arithmetic and copies ran while one was open for 3% of the time, Pallas kernels for 0%

profile of v1, /device:TPU:0, one launch (start us, length us, event | category | flops | bytes accessed | tf_op | source)
XLA Modules:
  0.0 128.5 jit_solution(17491638563863864280)
XLA Ops:
  7.2 1.3 stack.14
  8.4 7.7 %all-to-all-start = ((f32[8,2,128]{2,1,0:T(2,128)}), f32[8,2,128]{2,1,0:T(2,128)S(1)}, u32[]{:S(2)}, u32[]{:S(2)}) async-start(f32[8,2,128]{2,1,0:T(2,128)} %stack.14), calls=%async_computation | async-start | bytes 16384 | tf_op jit(solution)/shard_map/all_to_all | solution.py:65
  16.1 0.0 reduce-scatter.4.cloned.1.call-start
  16.2 0.0 copy-start.2
  16.2 0.0 copy-start.3
  16.2 1.4 %fusion.18 = (f32[2,2,4,4096]{3,2,1,0:T(4,128)S(1)}, f32[2,2,4,4096]{3,2,1,0:T(4,128)S(1)}) fusion(f32[1,2,8,4096]{3,2,1,0:T(8,128)} %bitcast.32, f32[1,2,8,4096]{3,2,1,0:T(8,128)} %bitcast.38), kind=kLoop, calls=%fused_computation.49 | loop fusion | flops 131072 | bytes 1048576 | tf_op jit(solution)/shard_map/stack | solution.py:62
  17.6 1.3 %collective-permute-start.3 = (f32[2,2,4,4096]{3,2,1,0:T(4,128)S(1)}, f32[2,2,4,4096]{3,2,1,0:T(4,128)S(1)}, u32[]{:S(2)}, u32[]{:S(2)}) collective-permute-start(f32[2,2,4,4096]{3,2,1,0:T(4,128)S(1)} %get-tuple-element.33), channel_id=1, source_target_pairs={{1,0},{2,1},{3,2},{4,3},{5,4},{6,5},{7,6},{8,7},{9,8},{10,9},{11,1... | collective-permute-start | bytes 786440 | tf_op jit(solution)/shard_map/ppermute | solution.py:18
  18.9 3.0 %collective-permute-start.2 = (f32[2,2,4,4096]{3,2,1,0:T(4,128)S(1)}, f32[2,2,4,4096]{3,2,1,0:T(4,128)S(1)}, u32[]{:S(2)}, u32[]{:S(2)}) collective-permute-start(f32[2,2,4,4096]{3,2,1,0:T(4,128)S(1)} %get-tuple-element.32), channel_id=1, source_target_pairs={{0,1},{1,2},{2,3},{3,4},{4,5},{5,6},{6,7},{7,8},{8,9},{9,10},{10,1... | collective-permute-start | bytes 786440 | tf_op jit(solution)/shard_map/ppermute | solution.py:18
  21.9 0.0 copy-start.4
  22.0 0.6 copy-done.4
  22.6 0.1 multiply_sine_fusion
  22.7 0.1 pad_subtract_fusion
  22.8 0.0 copy-done.2
  22.8 0.0 copy-done.3
  22.8 1.1 fusion.4
  23.9 0.0 all-to-all-done
  23.9 0.2 broadcast_in_dim.24
  24.1 0.3 broadcast_in_dim.25
  24.4 0.2 broadcast_in_dim.22
  24.6 0.3 broadcast_in_dim.23
  24.8 0.1 pad_slice_fusion.5
  24.9 0.1 multiply_add_fusion.2
  25.1 1.3 %collective-permute-start.1 = (f32[4,4096]{1,0:T(4,128)S(1)}, f32[4,4096]{1,0:T(4,128)S(1)}, u32[]{:S(2)}, u32[]{:S(2)}) collective-permute-start(f32[4,4096]{1,0:T(4,128)S(1)} %get-tuple-element.38), channel_id=1, source_target_pairs={{1,0},{2,1},{3,2},{4,3},{5,4},{6,5},{7,6},{8,7},{9,8},{10,9},{11,1... | collective-permute-start | bytes 196616 | tf_op jit(solution)/shard_map/ppermute | solution.py:18
  26.4 3.7 %collective-permute-start = (f32[4,4096]{1,0:T(4,128)S(1)}, f32[4,4096]{1,0:T(4,128)S(1)}, u32[]{:S(2)}, u32[]{:S(2)}) collective-permute-start(f32[4,4096]{1,0:T(4,128)S(1)} %get-tuple-element.37), channel_id=1, source_target_pairs={{0,1},{1,2},{2,3},{3,4},{4,5},{5,6},{6,7},{7,8},{8,9},{9,10},{10,1... | collective-permute-start | bytes 196616 | tf_op jit(solution)/shard_map/ppermute | solution.py:18
  30.1 0.1 pad_subtract_fusion.1
  30.2 0.0 copy-start
  30.2 0.0 copy-start.1
  30.2 0.0 collective-permute-done.1
  30.2 0.8 collective-permute-done
  31.0 0.1 broadcast_multiply_fusion.1
  31.1 0.0 collective-permute-done.3
  31.1 0.0 collective-permute-done.2
  31.1 0.0 copy-done
  31.2 0.1 copy-done.1
  31.2 0.3 add_multiply_fusion.6
  31.6 0.1 slice.290
  31.7 0.3 slice.292
  32.0 0.6 add_multiply_fusion.5
  32.6 0.9 add_multiply_fusion.4
  33.5 0.1 slice.294
  33.6 0.3 slice.296
  33.9 0.4 add_multiply_fusion.3
  34.4 1.0 add_multiply_fusion.2
  35.3 0.1 slice.298
  35.4 0.3 slice.300
  35.8 0.4 add_multiply_fusion.1
  36.2 1.1 add_multiply_fusion
  37.3 0.8 fusion.23
  38.1 0.1 fusion.19
  38.2 0.1 fusion.21
  38.3 0.4 multiply_reduce_fusion.5
  38.7 0.1 fusion.31
  38.8 0.5 add.288
  39.3 0.2 reduce_sum.259
  39.5 0.1 fusion.27
  39.6 0.5 add.283
  40.2 0.2 reduce_sum.253
  40.4 1.0 copy.8
  41.4 0.0 reduce-scatter.4.cloned.1.call-update
  41.5 78.8 %reduce-scatter.4.cloned.1.call-done = f32[128,2]{1,0:T(8,128)} async-done(((f32[1024,2]{1,0:T(8,128)}), f32[128,2]{1,0:T(8,128)}) %reduce-scatter.4.cloned.1.call-update) | async-done | bytes 1040
  120.2 1.5 %copy.9 = f32[2,128]{1,0:T(2,128)} copy(f32[2,128]{0,1:T(8,128)} %bitcast.46) | data formatting | bytes 2048
  (9 shorter events, 0.1 us)
Async XLA Ops:
  8.4 15.4 %all-to-all-start = ((f32[8,2,128]{2,1,0:T(2,128)}), f32[8,2,128]{2,1,0:T(2,128)S(1)}, u32[]{:S(2)}, u32[]{:S(2)}) async-start(f32[8,2,128]{2,1,0:T(2,128)} %stack.14), calls=%async_computation | async-start | bytes 16384 | tf_op jit(solution)/shard_map/all_to_all | solution.py:65
  16.1 104.1 %reduce-scatter.4.cloned.1.call-start = ((), (), s32[]{:S(2)}) async-start(), calls=%async_computation.2 | async-start | bytes 589824
  16.2 6.6 %copy-start.2 = (s32[4,8,4096]{2,1,0:T(8,128)S(1)}, s32[4,8,4096]{2,1,0:T(8,128)}, u32[]{:S(2)}) copy-start(s32[4,8,4096]{2,1,0:T(8,128)} %param.7) | copy-start | bytes 1572868
  16.2 6.6 %copy-start.3 = (bf16[4,8,4096]{2,1,0:T(8,128)(2,1)S(1)}, bf16[4,8,4096]{2,1,0:T(8,128)(2,1)}, u32[]{:S(2)}) copy-start(bf16[4,8,4096]{2,1,0:T(8,128)(2,1)} %param.8) | copy-start | bytes 786436
  17.6 13.6 %collective-permute-start.3 = (f32[2,2,4,4096]{3,2,1,0:T(4,128)S(1)}, f32[2,2,4,4096]{3,2,1,0:T(4,128)S(1)}, u32[]{:S(2)}, u32[]{:S(2)}) collective-permute-start(f32[2,2,4,4096]{3,2,1,0:T(4,128)S(1)} %get-tuple-element.33), channel_id=1, source_target_pairs={{1,0},{2,1},{3,2},{4,3},{5,4},{6,5},{7,6},{8,7},{9,8},{10,9},{11,1... | collective-permute-start | bytes 786440 | tf_op jit(solution)/shard_map/ppermute | solution.py:18
  18.9 12.3 %collective-permute-start.2 = (f32[2,2,4,4096]{3,2,1,0:T(4,128)S(1)}, f32[2,2,4,4096]{3,2,1,0:T(4,128)S(1)}, u32[]{:S(2)}, u32[]{:S(2)}) collective-permute-start(f32[2,2,4,4096]{3,2,1,0:T(4,128)S(1)} %get-tuple-element.32), channel_id=1, source_target_pairs={{0,1},{1,2},{2,3},{3,4},{4,5},{5,6},{6,7},{7,8},{8,9},{9,10},{10,1... | collective-permute-start | bytes 786440 | tf_op jit(solution)/shard_map/ppermute | solution.py:18
  21.9 0.7 copy-start.4
  25.1 5.1 %collective-permute-start.1 = (f32[4,4096]{1,0:T(4,128)S(1)}, f32[4,4096]{1,0:T(4,128)S(1)}, u32[]{:S(2)}, u32[]{:S(2)}) collective-permute-start(f32[4,4096]{1,0:T(4,128)S(1)} %get-tuple-element.38), channel_id=1, source_target_pairs={{1,0},{2,1},{3,2},{4,3},{5,4},{6,5},{7,6},{8,7},{9,8},{10,9},{11,1... | collective-permute-start | bytes 196616 | tf_op jit(solution)/shard_map/ppermute | solution.py:18
  26.4 4.6 %collective-permute-start = (f32[4,4096]{1,0:T(4,128)S(1)}, f32[4,4096]{1,0:T(4,128)S(1)}, u32[]{:S(2)}, u32[]{:S(2)}) collective-permute-start(f32[4,4096]{1,0:T(4,128)S(1)} %get-tuple-element.37), channel_id=1, source_target_pairs={{0,1},{1,2},{2,3},{3,4},{4,5},{5,6},{6,7},{7,8},{8,9},{9,10},{10,1... | collective-permute-start | bytes 196616 | tf_op jit(solution)/shard_map/ppermute | solution.py:18
  30.2 1.0 copy-start
  30.2 1.0 copy-start.1
Sparse Core Ops, SparseCore 0:
  41.6 78.5 reduce-scatter.3
